TPU v7x, 512 devices: a whole 4x4x16 slice. The times are simulated.
512 devices in a mesh: attn: 64 (over y, z), dp: 4 (over x), tensor: 2 (over core).
Axes of the slice: x: 4, y: 4, z: 16, core: 2. Of those that a mesh axis runs over, the one named last changes fastest.
Arguments:
- hidden_state: bfloat16 [256, 8192], P('dp', 'attn'), may hold values from -6 to 6
- w_query: bfloat16 [8192, 8192], P('attn', 'tensor'), may hold values from -0.0625 to 0.0625
- w_keyval: bfloat16 [8192, 2, 1024], P('attn', None, 'tensor'), may hold values from -0.0625 to 0.0625
- w_output: bfloat16 [8192, 8192], P('tensor', 'attn'), may hold values from -0.0625 to 0.0625
- kv_cache: bfloat16 [4, 49152, 2, 8, 128], P('dp', 'attn', None, 'tensor'), as said below
- lengths: int32 [4, 64], P('dp'), may hold values from 1 to 256, 8192 in all within a row
- owner_of: int32 [4, 64, 1], P('dp'), may hold values from 0 to 63; in each aligned block of 64 rows (0 to 63, 64 to 127, ..., all dimensions but the last counted through in order) at most 3 rows name the same one
Outputs:
- attended: bfloat16 [256, 8192], P('dp', 'attn')
Inputs may be any that keep to these rules, and one draw needn't show every extreme that they name: `owner_of`: in each data group at most 3 requests are placed on one attention device, and in some groups exactly 3 on one. The lengths of each data group sum to 8192, and the longest is exactly 256. `kv_cache`: finite keys and values.
All inputs are finite; a program needn't handle non-finite values.
Results may differ from a plain program's by a relative error of at most 0.009.
The roundings to bfloat16 on the way count: a program that leaves them out, or rounds other values in their place, can miss the bound.
Values may be sent and summed in bfloat16 or wider, within the bound.
No kernel may reach another device: no remote copies, remote signals or barrier semaphores. Data moves between devices by JAX's collectives and lax.ppermute only.
A program may use at most 64 MiB of HBM per device.

v0:
```python
import math
import jax
import jax.numpy as jnp
from jax import lax
from jax.sharding import PartitionSpec as P

HD = 128
CAP = 3
ROPE_BASE = 500000.0


def rotate_pairs(vectors, positions):
    half_dim = vectors.shape[-1] // 2
    steps_f = jnp.arange(half_dim).astype(jnp.float32) * (2.0 / vectors.shape[-1])
    inv_freq = jnp.exp(-math.log(ROPE_BASE) * steps_f)
    angles = positions[:, None] * inv_freq[None, :]
    cosine = jnp.cos(angles)[:, None, :]
    sine_part = jnp.sin(angles)[:, None, :]
    front_half = vectors[..., :half_dim]
    back_half = vectors[..., half_dim:]
    return jnp.concatenate(
        [front_half * cosine - back_half * sine_part, back_half * cosine + front_half * sine_part],
        axis=-1,
    )


def finish(query_part, keyval_part, positions, heads_loc, kv_loc):
    row_count = query_part.shape[0]
    query_rot = rotate_pairs(query_part.reshape(row_count, heads_loc, HD), positions).astype(
        jnp.bfloat16
    )
    keyval = keyval_part.reshape(row_count, 2, kv_loc, HD)
    key_rot = rotate_pairs(keyval[:, 0], positions).astype(jnp.bfloat16)
    val_new = keyval[:, 1].astype(jnp.bfloat16)
    packed = jnp.stack([key_rot, val_new], axis=1).reshape(row_count, 2 * kv_loc * HD)
    return (query_rot.reshape(row_count, heads_loc * HD), packed)


def local(hidden_state, w_query, w_keyval, w_output, kv_cache, lengths, owner_of):
    rows_group = hidden_state.shape[0]
    width_loc = hidden_state.shape[1]
    my_index = lax.axis_index("attn")
    heads_loc = w_query.shape[1] // HD
    kv_loc = w_keyval.shape[2] // HD
    group_size = heads_loc // kv_loc
    score_scale = 1.0 / math.sqrt(HD)
    query_part = jnp.dot(hidden_state, w_query, preferred_element_type=jnp.float32)
    keyval_part = jnp.dot(
        hidden_state,
        w_keyval.reshape(width_loc, 2 * kv_loc * HD),
        preferred_element_type=jnp.float32,
    )
    owners = owner_of.reshape(rows_group)
    req_lens = lengths.reshape(rows_group)
    req_order = jnp.arange(rows_group, dtype=jnp.int32)
    same_owner = owners[:, None] == owners[None, :]
    earlier = req_order[None, :] < req_order[:, None]
    before_mine = same_owner & earlier
    starts = jnp.sum(jnp.where(before_mine, req_lens[None, :], 0), axis=1)
    slot_rank = jnp.sum(before_mine.astype(jnp.int32), axis=1)
    positions = req_lens.astype(jnp.float32)
    query_sum, keyval_sum = lax.psum((query_part, keyval_part), "attn")
    query_rows, keyval_rows = finish(query_sum, keyval_sum, positions, heads_loc, kv_loc)
    slot_hit = (owners[None, :] == my_index) & (
        slot_rank[None, :] == jnp.arange(CAP, dtype=jnp.int32)[:, None]
    )
    chosen = jnp.sum(jnp.where(slot_hit, req_order[None, :], 0), axis=1)
    present = jnp.any(slot_hit, axis=1)
    my_start = jnp.take(starts, chosen)
    my_len = jnp.where(present, jnp.take(req_lens, chosen), 0)
    query_mine = jnp.take(query_rows, chosen, axis=0)
    keyval_mine = jnp.take(keyval_rows, chosen, axis=0).reshape(CAP, 2, kv_loc, HD)
    cache_local = kv_cache[0]
    grouped = query_mine.reshape(CAP, kv_loc, group_size, HD)
    scores = (
        jnp.einsum("ckgd,skd->ckgs", grouped, cache_local[:, 0], preferred_element_type=jnp.float32)
        * score_scale
    )
    own_score = (
        jnp.einsum("ckgd,ckd->ckg", grouped, keyval_mine[:, 0], preferred_element_type=jnp.float32)
        * score_scale
    )
    slot_pos = jnp.arange(cache_local.shape[0], dtype=jnp.int32)
    live = (slot_pos[None, :] >= my_start[:, None]) & (
        slot_pos[None, :] < (my_start + my_len)[:, None]
    )
    live = live[:, None, None, :]
    row_max = jnp.maximum(jnp.max(jnp.where(live, scores, -jnp.inf), axis=-1), own_score)
    weights = jnp.where(live, jnp.exp(scores - row_max[..., None]), 0.0)
    own_weight = jnp.exp(own_score - row_max)
    total_weight = jnp.sum(weights, axis=-1) + own_weight
    probs = (weights / total_weight[..., None]).astype(jnp.bfloat16)
    own_prob = (own_weight / total_weight).astype(jnp.bfloat16)
    mixed = jnp.einsum(
        "ckgs,skd->ckgd", probs, cache_local[:, 1], preferred_element_type=jnp.float32
    )
    mixed = (
        mixed
        + own_prob.astype(jnp.float32)[..., None]
        * keyval_mine[:, 1].astype(jnp.float32)[:, :, None, :]
    )
    out_slots = mixed.reshape(CAP, heads_loc * HD).astype(jnp.bfloat16)
    gathered = lax.all_gather(out_slots, "attn", axis=0, tiled=True)
    heads_out = jnp.take(gathered, owners * CAP + slot_rank, axis=0)
    out_part = jnp.dot(heads_out, w_output, preferred_element_type=jnp.float32)
    out_total = lax.psum(out_part, "tensor")
    return out_total.astype(jnp.bfloat16)


def solution(mesh):
    placed = (
        P("dp", "attn"),
        P("attn", "tensor"),
        P("attn", None, "tensor"),
        P("tensor", "attn"),
        P("dp", "attn", None, "tensor", None),
        P("dp", None),
        P("dp", None, None),
    )
    return jax.shard_map(
        local, mesh=mesh, in_specs=placed, out_specs=P("dp", "attn"), check_vma=False
    )
```

profile of v0, /device:TPU:1, one launch (start us, length us, event | category | flops | bytes accessed | tf_op | source)
XLA Modules:
  0.0 454.5 jit_solution(9612542293275163695)
XLA Ops:
  6.5 0.0 copy-start
  6.5 0.0 all-reduce.3.cloned.1.call-start
  6.5 1.2 copy-done
  7.8 1.0 convolution_bitcast_fusion
  8.8 0.0 copy-start.5
  8.8 0.0 copy-start.6
  8.8 1.2 copy.37
  10.0 0.0 copy-start.1
  10.0 0.0 copy-start.7
  10.0 0.0 copy-done.5
  10.0 0.0 copy-done.6
  10.0 0.2 fusion.30
  10.2 0.0 copy-start.4
  10.2 0.8 reshape.238
  11.0 0.0 all-reduce.3.cloned.1.call-update
  11.1 0.0 all-gather.3.cloned.1.call-start
  11.1 0.0 copy-done.1
  11.1 0.0 copy-done.7
  11.1 0.2 select_reduce_fusion.1
  11.3 0.1 select_reduce_fusion.2
  11.5 0.6 gather_fusion.4
  12.1 0.6 gather_fusion.3
  12.8 0.0 copy-done.4
  12.8 1.4 copy.65
  14.1 0.1 fusion.24
  14.3 0.1 fusion.17
  14.4 0.2 multiply_cosine_fusion
  14.6 269.9 %all-reduce.3.cloned.1.call-done = (f32[64,32,128]{2,1,0:T(8,128)}, f32[64,2,4,128]{3,2,1,0:T(4,128)}) async-done(((f32[64,32,128]{2,1,0:T(8,128)}, f32[64,2,4,128]{3,2,1,0:T(4,128)}), (f32[64,32,128]{2,1,0:T(8,128)}, f32[64,2,4,128]{3,2,1,0:T(4,128)})) %all-reduce.3.cloned.1.call-update) | async-done | bytes 1310736 | tf_op jit(solution)/shard_map/psum | solution.py:62
  284.5 0.0 copy-start.2
  284.5 1.0 slice_bitcast_fusion.4
  285.5 0.9 slice.87
  286.4 0.2 fusion.12
  286.6 0.1 pad_maximum_fusion.1
  286.7 0.1 reshape.239
  286.8 0.6 gather_fusion.1
  287.4 0.1 broadcast_select_fusion
  287.5 0.0 copy-done.2
  287.5 0.5 subtract_convert_fusion
  287.9 0.0 copy-start.3
  288.0 0.3 pad_maximum_fusion
  288.3 0.2 copy.66
  288.5 0.6 gather_fusion
  289.1 0.1 copy_select_fusion
  289.1 0.1 fusion.15
  289.3 0.1 copy-done.3
  289.4 0.4 select_reduce_fusion
  289.8 0.2 fusion.7
  290.0 0.3 fusion.2
  290.3 0.6 reshape.283
  290.9 0.0 all-gather.3.cloned.1.call-update
  291.0 136.5 %all-gather.3.cloned.1.call-done = bf16[64,3,4096]{2,1,0:T(4,128)(2,1)} async-done(((bf16[1,3,4096]{2,1,0:T(4,128)(2,1)}), bf16[64,3,4096]{2,1,0:T(4,128)(2,1)}) %all-gather.3.cloned.1.call-update) | async-done | bytes 1572880 | tf_op jit(solution)/shard_map/all_gather | solution.py:103
  427.5 3.1 reshape.284
  430.6 0.9 gather_fusion.2
  431.5 1.6 fusion.3
  433.1 14.6 %psum.23 = bf16[64,128]{1,0:T(8,128)(2,1)} all-reduce(f32[64,128]{1,0:T(8,128)S(1)} %fusion.3), channel_id=1, replica_groups=mesh['attn'=64,'dp'=4,'tensor'=2] {'tensor'}, use_global_device_ids=true, to_apply=%region_8.10 | all-reduce | flops 8192 | bytes 49152 | tf_op jit(solution)/shard_map/psum | solution.py:106
  (16 shorter events, 0.1 us)
Async XLA Ops:
  6.5 1.2 copy-start
  6.5 277.9 %all-reduce.3.cloned.1.call-start = ((), (), s32[]{:S(2)}) async-start(), calls=%async_computation.1 | async-start | bytes 2621440 | tf_op jit(solution)/shard_map/psum | solution.py:62
  8.8 1.2 copy-start.5
  8.8 1.2 copy-start.6
  10.0 1.1 copy-start.1
  10.0 1.2 copy-start.7
  10.2 2.6 copy-start.4
  11.1 416.4 %all-gather.3.cloned.1.call-start = ((), (), s32[]{:S(2)}) async-start(), calls=%async_computation | async-start | bytes 2129920 | tf_op jit(solution)/shard_map/all_gather | solution.py:103
  284.5 3.0 copy-start.2
  287.9 1.4 copy-start.3
Sparse Core Ops, SparseCore 0:
  11.2 273.2 all-reduce.2
  291.1 136.3 all-gather.2
where the time goes:
time: 455 us
  waiting for transfers between devices  406 us (89%)
  blocking collectives  14.6 us (3%)
  local copies, waits for them, and re-layouts  14 us (3%)
  between operations  13.7 us (3%)
    psum x1, waiting for transfers between devices, local(): query_sum, keyval_sum = lax.psum((query_part, keyval_part), 'attn')  270 us
    all_gather x1, waiting for transfers between devices, local(): gathered = lax.all_gather(out_slots, 'attn', axis=0, tiled=True)  137 us
    psum x1, blocking collectives, local(): out_total = lax.psum(out_part, 'tensor')  14.6 us
  transfers between devices with their start and end apart: 2, of which 2 were waited for; matrix products, arithmetic and copies ran while one was open for 1% of the time, Pallas kernels for 0%

commit v1 on v0

--- a/solution.py
+++ b/solution.py
@@ -3,10 +3,14 @@
 import jax.numpy as jnp
 from jax import lax
 from jax.sharding import PartitionSpec as P
+from jax.lax import all_to_all, axis_size
 
 HD = 128
 CAP = 3
 ROPE_BASE = 500000.0
+convert_screen = lambda axis_id, load: jnp.concatenate(
+    all_to_all(jnp.stack([load] * axis_size(axis_id)), axis_id, 0, 0), axis=0
+)
 
 
 def rotate_pairs(vectors, positions):
@@ -100,7 +104,7 @@
         * keyval_mine[:, 1].astype(jnp.float32)[:, :, None, :]
     )
     out_slots = mixed.reshape(CAP, heads_loc * HD).astype(jnp.bfloat16)
-    gathered = lax.all_gather(out_slots, "attn", axis=0, tiled=True)
+    gathered = convert_screen("attn", out_slots)
     heads_out = jnp.take(gathered, owners * CAP + slot_rank, axis=0)
     out_part = jnp.dot(heads_out, w_output, preferred_element_type=jnp.float32)
     out_total = lax.psum(out_part, "tensor")

time: 455 us -> 416 us (0.914)
  waiting for transfers between devices: 406 us -> 352 us
  starting transfers between devices: 0.04 us -> 9.05 us
    all_gather x1 -> x0, waiting for transfers between devices: 137 us -> none  [local(): gathered = lax.all_gather(out_slots, 'attn', axis=0, tiled=True)]
    all_to_all x0 -> x1, waiting for transfers between devices: none -> 82.3 us  [all_to_all(jnp.stack([load] * axis_size(axis_id)), axis_id, 0, 0)]
    all_to_all x0 -> x1, starting transfers between devices: none -> 9.05 us  [all_to_all(jnp.stack([load] * axis_size(axis_id)), axis_id, 0, 0)]
where the time goes in v1:
time: 416 us
  waiting for transfers between devices  352 us (85%)
  blocking collectives  19.1 us (5%)
  local copies, waits for them, and re-layouts  15.7 us (4%)
  between operations  13.7 us (3%)
  starting transfers between devices  9.05 us (2%)
    psum x1, waiting for transfers between devices, local(): query_sum, keyval_sum = lax.psum((query_part, keyval_part), 'attn')  270 us
    all_to_all x1, waiting for transfers between devices, all_to_all(jnp.stack([load] * axis_size(axis_id)), axis_id, 0, 0)  82.3 us
    psum x1, blocking collectives, local(): out_total = lax.psum(out_part, 'tensor')  19.1 us
    all_to_all x1, starting transfers between devices, all_to_all(jnp.stack([load] * axis_size(axis_id)), axis_id, 0, 0)  9.05 us
  transfers between devices with their start and end apart: 2, of which 2 were waited for; matrix products, arithmetic and copies ran while one was open for 1% of the time, Pallas kernels for 0%

profile of v1, /device:TPU:1, one launch (start us, length us, event | category | flops | bytes accessed | tf_op | source)
XLA Modules:
  0.0 415.6 jit_solution(16606112919233886089)
XLA Ops:
  6.5 0.0 copy-start
  6.5 0.0 all-reduce.3.cloned.1.call-start
  6.5 1.2 copy-done
  7.8 1.0 convolution_bitcast_fusion
  8.8 0.0 copy-start.5
  8.8 0.0 copy-start.6
  8.8 1.2 copy.31
  10.0 0.0 copy-start.1
  10.0 0.0 copy-start.7
  10.0 0.0 copy-done.5
  10.0 0.0 copy-done.6
  10.0 0.2 fusion.30
  10.2 0.0 copy-start.4
  10.2 0.8 reshape.244
  11.0 0.0 all-reduce.3.cloned.1.call-update
  11.1 0.0 copy-done.1
  11.1 0.0 copy-done.7
  11.1 0.2 select_reduce_fusion.1
  11.3 0.1 select_reduce_fusion.2
  11.4 0.6 gather_fusion.4
  12.1 0.6 gather_fusion.3
  12.7 0.0 copy-done.4
  12.7 1.4 copy.62
  14.1 0.1 fusion.24
  14.3 0.1 fusion.17
  14.3 0.2 multiply_cosine_fusion
  14.5 269.9 %all-reduce.3.cloned.1.call-done = (f32[64,32,128]{2,1,0:T(8,128)}, f32[64,2,4,128]{3,2,1,0:T(4,128)}) async-done(((f32[64,32,128]{2,1,0:T(8,128)}, f32[64,2,4,128]{3,2,1,0:T(4,128)}), (f32[64,32,128]{2,1,0:T(8,128)}, f32[64,2,4,128]{3,2,1,0:T(4,128)})) %all-reduce.3.cloned.1.call-update) | async-done | bytes 1310736 | tf_op jit(solution)/shard_map/psum | solution.py:66
  284.4 0.0 copy-start.2
  284.4 1.0 slice_bitcast_fusion.4
  285.4 0.9 slice.87
  286.4 0.2 fusion.12
  286.5 0.1 pad_maximum_fusion.1
  286.7 0.1 reshape.245
  286.8 0.6 gather_fusion.1
  287.3 0.1 broadcast_select_fusion
  287.4 0.0 copy-done.2
  287.4 0.5 subtract_convert_fusion
  287.9 0.0 copy-start.3
  287.9 0.3 pad_maximum_fusion
  288.2 0.2 copy.63
  288.4 0.6 gather_fusion
  289.0 0.1 copy_select_fusion
  289.1 0.1 fusion.15
  289.2 0.1 copy-done.3
  289.3 0.4 select_reduce_fusion
  289.7 0.2 fusion.7
  290.0 0.3 fusion.2
  290.3 2.3 stack.5
  292.6 9.1 %all-to-all-start = ((bf16[64,3,4096]{2,1,0:T(4,128)(2,1)}), bf16[64,3,4096]{2,1,0:T(4,128)(2,1)}, u32[]{:S(2)}, u32[]{:S(2)}) async-start(bf16[64,3,4096]{2,1,0:T(4,128)(2,1)} %stack.5), calls=%async_computation | async-start | bytes 4194304 | tf_op jit(solution)/shard_map/all_to_all | solution.py:12
  301.7 82.3 %all-to-all-done = bf16[64,3,4096]{2,1,0:T(4,128)(2,1)} async-done(((bf16[64,3,4096]{2,1,0:T(4,128)(2,1)}), bf16[64,3,4096]{2,1,0:T(4,128)(2,1)}, u32[]{:S(2)}, u32[]{:S(2)}) %all-to-all-start) | async-done | bytes 1572896 | tf_op jit(solution)/shard_map/all_to_all | solution.py:12
  384.0 3.1 reshape.246
  387.2 0.9 gather_fusion.2
  388.1 1.6 fusion.3
  389.7 19.1 %psum.23 = bf16[64,128]{1,0:T(8,128)(2,1)} all-reduce(f32[64,128]{1,0:T(8,128)S(1)} %fusion.3), channel_id=1, replica_groups=mesh['attn'=64,'dp'=4,'tensor'=2] {'tensor'}, use_global_device_ids=true, to_apply=%region_8.10 | all-reduce | flops 8192 | bytes 49152 | tf_op jit(solution)/shard_map/psum | solution.py:110
  (17 shorter events, 0.2 us)
Async XLA Ops:
  6.5 1.2 copy-start
  6.5 277.9 %all-reduce.3.cloned.1.call-start = ((), (), s32[]{:S(2)}) async-start(), calls=%async_computation.1 | async-start | bytes 2621440 | tf_op jit(solution)/shard_map/psum | solution.py:66
  8.8 1.2 copy-start.5
  8.8 1.2 copy-start.6
  10.0 1.1 copy-start.1
  10.0 1.1 copy-start.7
  10.2 2.5 copy-start.4
  284.4 3.0 copy-start.2
  287.9 1.4 copy-start.3
  292.6 91.4 %all-to-all-start = ((bf16[64,3,4096]{2,1,0:T(4,128)(2,1)}), bf16[64,3,4096]{2,1,0:T(4,128)(2,1)}, u32[]{:S(2)}, u32[]{:S(2)}) async-start(bf16[64,3,4096]{2,1,0:T(4,128)(2,1)} %stack.5), calls=%async_computation | async-start | bytes 4194304 | tf_op jit(solution)/shard_map/all_to_all | solution.py:12
Sparse Core Ops, SparseCore 0:
  11.2 273.1 all-reduce.2
